TPU v7x, 32 devices: a whole 2x2x4 slice. The times are simulated.
32 devices in a mesh: exp: 4 (over z), row: 4 (over y, core), col: 2 (over x).
Axes of the slice: x: 2, y: 2, z: 4, core: 2. Of those that a mesh axis runs over, the one named last changes fastest.
Arguments:
- exposures: float32 [64, 128, 1024], P('exp', 'row', 'col'), may hold values from -6 to 6
- bad_pixels: int32 [64, 128, 1024], P('exp', 'row', 'col'), may hold values 0 or 1
- offsets: int32 [64, 2], P('exp'), may hold values from -8 to 8, as said below
- warp_index: int32 [64, 2], P('exp'), may hold values from 0 to 15
- blur_index: int32 [64], P('exp'), may hold values from 0 to 7
Outputs:
- residual: float32 [64, 128, 1024], P('exp', 'row', 'col')
- median_sky: float32 [128, 1024], P('row', 'col')
Inputs may be any that keep to these rules, and one draw needn't show every extreme that they name: `offsets`: in each component some exposure has the offset -8 and some has 8.
All inputs are finite; a program needn't handle non-finite values. No bound on the sum of `bad_pixels` on one device may be relied on, other than what follows from the above.
Results may differ from a plain program's by a relative error of at most 0.0003.
Values sent between devices are 32-bit elements; how exact they have to be, the bound alone decides.
No kernel may reach another device: no remote copies, remote signals or barrier semaphores. Data moves between devices by JAX's collectives and lax.ppermute only.
A program may use at most 64 MiB of HBM per device.

v0:
```python
import jax
import jax.numpy as jnp
from jax import lax
from jax.sharding import PartitionSpec as P

NFRAC = 16
NPSF = 8
PSF_RADIUS = 4
PASSES = 16
HALO = 11
sentinel = 1000000.0
half_sentinel = 500000.0
pivot_span = 16.0


def _row_halo(block, dim, width):
    count = lax.axis_size("row")
    forward = [(i, i + 1) for i in range(count - 1)]
    backward = [(target, source) for source, target in forward]
    size = block.shape[dim]
    low = lax.ppermute(lax.slice_in_dim(block, size - width, None, axis=dim), "row", forward)
    high = lax.ppermute(lax.slice_in_dim(block, 0, width, axis=dim), "row", backward)
    return jnp.concatenate([low, block, high], axis=dim)


def _col_halo(block, dim, width):
    count = lax.axis_size("col")
    size = block.shape[dim]
    right_edge = lax.slice_in_dim(block, size - width, None, axis=dim)
    left_edge = lax.slice_in_dim(block, 0, width, axis=dim)
    if count != 2:
        forward = [(i, i + 1) for i in range(count - 1)]
        backward = [(target, source) for source, target in forward]
        low = lax.ppermute(right_edge, "col", forward)
        high = lax.ppermute(left_edge, "col", backward)
        return jnp.concatenate([low, block, high], axis=dim)
    first = lax.axis_index("col") == 0
    outgoing = jnp.moveaxis(jnp.where(first, right_edge, left_edge), dim, 0)
    packed_shape = outgoing.shape
    packed = outgoing.reshape(width, -1)
    arrived = lax.ppermute(packed, "col", [(0, 1), (1, 0)])
    arrived = jnp.moveaxis(arrived.reshape(packed_shape), 0, dim)
    zeros = jnp.zeros_like(arrived)
    low = jnp.where(first, zeros, arrived)
    high = jnp.where(first, arrived, zeros)
    return jnp.concatenate([low, block, high], axis=dim)


def extended(block, row_dim, col_dim, width):
    return _col_halo(_row_halo(block, row_dim, width), col_dim, width)


def lanczos_table():
    fraction = jnp.arange(NFRAC, dtype=jnp.float32) / NFRAC
    offset_grid = jnp.arange(-2, 4, dtype=jnp.float32)
    spread = offset_grid[None, :] - fraction[:, None]
    kernel = jnp.sinc(spread) * jnp.sinc(spread / 3.0)
    return kernel / jnp.sum(kernel, axis=1, keepdims=True)


def blur_table():
    offset_grid = jnp.arange(-PSF_RADIUS, PSF_RADIUS + 1, dtype=jnp.float32)
    widths = 0.7 + 0.2 * jnp.arange(NPSF, dtype=jnp.float32)
    kernel = jnp.exp(-0.5 * (offset_grid[None, :] / widths[:, None]) ** 2)
    return kernel / jnp.sum(kernel, axis=1, keepdims=True)


def lookup(indices, entries, kernel_table):
    chooser = (indices[:, None] == lax.broadcasted_iota(jnp.int32, (1, entries), 1)).astype(
        jnp.float32
    )
    return jnp.dot(chooser, kernel_table, precision=lax.Precision.HIGHEST)


def placed_taps(weights, shifts):
    reach = 2 * HALO + 1
    positions = lax.broadcasted_iota(jnp.int32, (1, 1, reach), 2)
    tap_slot = HALO + shifts[:, None, None] + lax.broadcasted_iota(jnp.int32, (1, 6, 1), 1) - 2
    spread = (tap_slot == positions).astype(jnp.float32)
    return jnp.sum(weights[:, :, None] * spread, axis=1)


def resample_axis(stack, coefficients, out_len, which_axis):
    out_shape = list(stack.shape)
    out_shape[which_axis] = out_len
    total = jnp.zeros(tuple(out_shape), jnp.float32)
    for position in range(2 * HALO + 1):
        window = lax.slice_in_dim(stack, position, position + out_len, 1, which_axis)
        total = total + coefficients[:, position, None, None] * window
    return total


def bisect_lower(valid_count, count_below):

    def one_pass(sweep_no, bounds):
        lower_edge, upper_edge = bounds
        middle = 0.5 * (lower_edge + upper_edge)
        enough = 2.0 * count_below(middle) >= valid_count
        return (jnp.where(enough, lower_edge, middle), jnp.where(enough, middle, upper_edge))

    initial = (
        jnp.full(valid_count.shape, -pivot_span, jnp.float32),
        jnp.full(valid_count.shape, pivot_span, jnp.float32),
    )
    return lax.fori_loop(0, PASSES, one_pass, initial)[0]


def stack_median(pixel_stack):
    valid_count = jnp.sum(pixel_stack < half_sentinel, axis=0, dtype=jnp.float32)

    def count_below(middle):
        return jnp.sum(pixel_stack <= middle[None], axis=0, dtype=jnp.float32)

    lower_edge = bisect_lower(valid_count, count_below)
    return jnp.min(jnp.where(pixel_stack > lower_edge[None], pixel_stack, sentinel), axis=0)


def body(exposures, bad_pixels, offsets, warp_index, blur_index):
    group_size, row_count, col_count = exposures.shape
    kernel_table = lanczos_table()
    coef_down = placed_taps(lookup(warp_index[:, 0], NFRAC, kernel_table), offsets[:, 0])
    coef_across = placed_taps(lookup(warp_index[:, 1], NFRAC, kernel_table), offsets[:, 1])
    padded = extended(exposures, 1, 2, HALO)
    across = resample_axis(padded, coef_down, row_count, 1)
    warped = resample_axis(across, coef_across, col_count, 2)
    flagged = jnp.where(bad_pixels == 1, sentinel, warped)
    band = stack_median(lax.all_to_all(flagged, "exp", split_axis=1, concat_axis=0, tiled=True))
    groups = lax.axis_size("exp")
    median_sky = lax.all_to_all(
        jnp.tile(band, (groups, 1)), "exp", split_axis=0, concat_axis=0, tiled=True
    )
    bordered = extended(median_sky, 0, 1, PSF_RADIUS)
    blur = blur_table()
    taps = 2 * PSF_RADIUS + 1
    blurred_rows = jnp.zeros((NPSF, row_count, col_count + 2 * PSF_RADIUS), jnp.float32)
    for tap_no in range(taps):
        blurred_rows = (
            blurred_rows
            + blur[:, tap_no, None, None] * bordered[None, tap_no : tap_no + row_count, :]
        )
    smoothed = jnp.zeros((NPSF, row_count, col_count), jnp.float32)
    for tap_no in range(taps):
        smoothed = (
            smoothed + blur[:, tap_no, None, None] * blurred_rows[:, :, tap_no : tap_no + col_count]
        )
    chooser = (blur_index[:, None] == lax.broadcasted_iota(jnp.int32, (1, NPSF), 1)).astype(
        jnp.float32
    )
    sky_model = jnp.zeros((group_size, row_count, col_count), jnp.float32)
    for kernel_no in range(NPSF):
        sky_model = sky_model + chooser[:, kernel_no, None, None] * smoothed[kernel_no][None]
    residual = jnp.where(bad_pixels == 1, 0.0, warped - sky_model)
    return (residual, median_sky)


def solution(mesh):
    return jax.shard_map(
        body,
        mesh=mesh,
        in_specs=(
            P("exp", "row", "col"),
            P("exp", "row", "col"),
            P("exp", None),
            P("exp", None),
            P("exp"),
        ),
        out_specs=(P("exp", "row", "col"), P("row", "col")),
        check_vma=False,
    )
```

profile of v0, /device:TPU:0, one launch (start us, length us, event | category | flops | bytes accessed | tf_op | source)
XLA Modules:
  0.0 90.9 jit_solution(72379477720639308)
XLA Ops:
  0.6 1.3 %fusion.134 = (f32[16,11,512]{2,1,0:T(8,128)S(1)}, f32[16,11,512]{2,1,0:T(8,128)S(1)}) fusion(f32[16,32,512]{2,1,0:T(8,128)} %param.8), kind=kLoop, calls=%fused_computation.315 | loop fusion | bytes 1441792 | tf_op jit(solution)/shard_map/slice | solution.py:22
  2.2 3.3 %collective-permute-start = (f32[16,11,512]{2,0,1:T(8,128)S(1)}, f32[16,11,512]{2,0,1:T(8,128)}, u32[]{:S(2)}, u32[]{:S(2)}) collective-permute-start(f32[16,11,512]{2,0,1:T(8,128)S(1)} %copy.47), channel_id=1, source_target_pairs={{0,2},{2,4},{4,6},{1,3},{3,5},{5,7},{8,10},{10,12},{12,14},{9,11},... | collective-permute-start | bytes 1081352 | tf_op jit(solution)/shard_map/ppermute | solution.py:21
  5.7 1.3 %collective-permute-start.1 = (f32[16,11,512]{2,0,1:T(8,128)S(1)}, f32[16,11,512]{2,0,1:T(8,128)S(1)}, u32[]{:S(2)}, u32[]{:S(2)}) collective-permute-start(f32[16,11,512]{2,0,1:T(8,128)S(1)} %copy.48), channel_id=1, source_target_pairs={{2,0},{4,2},{6,4},{3,1},{5,3},{7,5},{10,8},{12,10},{14,12},{11,9},... | collective-permute-start | bytes 1081352 | tf_op jit(solution)/shard_map/ppermute | solution.py:22
  7.7 0.8 slice_reduce_fusion.43
  8.5 1.1 %slice_reduce_fusion.44 = (f32[16]{0:T(128)}, f32[16]{0:T(128)}, f32[16]{0:T(128)}, f32[16]{0:T(128)}, f32[16]{0:T(128)}, /*index=5*/f32[16]{0:T(128)}, f32[16]{...) fusion(f32[16,23]{1,0:T(8,128)S(1)} %select_reduce_fusion), kind=kLoop, calls=%fused_computation.204 | loop fusion | bytes 2432 | tf_op jit(solution)/shard_map/slice | solution.py:89
  9.7 1.1 %slice_reduce_fusion.45 = (f32[16]{0:T(128)S(1)}, f32[16]{0:T(128)S(1)}, f32[16]{0:T(128)}, f32[16]{0:T(128)}, f32[16]{0:T(128)}, /*index=5*/f32[16]{0:T(128)}, ...) fusion(f32[16,23]{1,0:T(8,128)S(1)} %select_reduce_fusion.1), kind=kLoop, calls=%fused_computation.205 | loop fusion | bytes 2432 | tf_op jit(solution)/shard_map/slice | solution.py:89
  10.7 1.0 %constant_dynamic-update-slice_fusion.2 = f32[16,54,512]{2,0,1:T(8,128)S(1)} fusion(f32[16,11,512]{2,0,1:T(8,128)} %collective-permute-done), kind=kLoop, calls=%fused_computation.208 | loop fusion | bytes 720896
  13.0 2.4 %collective-permute-start.2 = (f32[11,864]{1,0:T(8,128)S(1)}, f32[11,864]{1,0:T(8,128)S(1)}, u32[]{:S(2)}, u32[]{:S(2)}) collective-permute-start(f32[11,864]{1,0:T(8,128)S(1)} %reshape.187), channel_id=1, source_target_pairs={{0,1},{1,0},{2,3},{3,2},{4,5},{5,4},{6,7},{7,6},{8,9},{9,8},{10,11... | collective-permute-start | bytes 114056 | tf_op jit(solution)/shard_map/ppermute | solution.py:41
  15.6 1.9 %collective-permute-done.2 = f32[11,864]{1,0:T(8,128)S(1)} collective-permute-done((f32[11,864]{1,0:T(8,128)S(1)}, f32[11,864]{1,0:T(8,128)S(1)}, u32[]{:S(2)}, u32[]{:S(2)}) %collective-permute-start.2) | collective-permute-done | bytes 38048 | tf_op jit(solution)/shard_map/ppermute | solution.py:41
  18.6 0.7 pad_maximum_fusion
  19.8 3.9 %fusion = f32[16,32,534]{2,0,1:T(8,128)S(1)} fusion(f32[16,54,534]{2,0,1:T(8,128)S(1)} %pad_maximum_fusion, f32[16]{0:T(128)S(1)} %copy-done.24, f32[16]{0:T(128)S(1)} %copy-done.25, f32[16]{0:T(128)S(1)} %copy-done.26, f32[16]{0:T(128)S(1)} %copy-done.27, f32[16]{0:T(128)S(1)} %copy-done.28, f32[16]{0:T(128)S(1)} %copy-done.29, f32[16]{0:T(128)S(1)} %copy-done.30, ...), kind=kLoop, calls=%fused_computation.8 | loop fusion | flops 12303360 | bytes 26248640 | tf_op jit(solution)/shard_map/add | solution.py:89
  23.8 7.0 %broadcast_select_fusion = (f32[16,32,512]{2,0,1:T(8,128)}, f32[16,32,512]{2,0,1:T(8,128)S(1)}, pred[16,32,512]{2,0,1:T(8,128)(4,1)S(1)}) fusion(f32[16,32,534]{2,0,1:T(8,128)S(1)} %fusion, f32[16]{0:T(128)S(1)} %get-tuple-element.56, f32[16]{0:T(128)S(1)} %copy-done.2, f32[16]{0:T(128)S(1)} %copy-done.3, f32[16]{0:T(128)S(1)} %copy-done.4, ...), kind=kLoop, calls=%fused_computation.119 | loop fusion | flops 12320768 | bytes 27526592 | tf_op jit(solution)/shard_map/jit(_where)/select_n | solution.py:126
  30.8 5.4 %all-to-all-start = ((f32[16,32,512]{2,0,1:T(8,128)}), f32[16,32,512]{2,0,1:T(8,128)S(1)}, u32[]{:S(2)}, u32[]{:S(2)}) async-start(f32[16,32,512]{2,0,1:T(8,128)} %get-tuple-element.113), calls=%async_computation | async-start | bytes 2097152 | tf_op jit(solution)/shard_map/all_to_all | solution.py:127
  36.4 26.2 %all-to-all-done = f32[16,32,512]{2,0,1:T(8,128)S(1)} async-done(((f32[16,32,512]{2,0,1:T(8,128)}), f32[16,32,512]{2,0,1:T(8,128)S(1)}, u32[]{:S(2)}, u32[]{:S(2)}) %all-to-all-start) | async-done | bytes 1048608 | tf_op jit(solution)/shard_map/all_to_all | solution.py:127
  63.4 3.6 %while.13 = (s32[]{:T(128)}, f32[8,512]{1,0:T(8,128)S(1)}, f32[8,512]{1,0:T(8,128)S(1)}, f32[64,8,512]{2,1,0:T(8,128)S(1)}, f32[8,512]{1,0:T(8,128)S(1)}, /*index=5*/s32[]{:T(128)}, s32[]{:T(128)}) while((s32[]{:T(128)}, f32[8,512]{1,0:T(8,128)S(1)}, f32[8,512]{1,0:T(8,128)S(1)}, f32[64,8,512]{2,1,0:T(8,128)S(1)}, ...), condition=%wide.region_7.9_spmd.clone, body=%wide.region_5.8_spmd.clone.sunk | while | flops 1110019 | bytes 1302625 | solution.py:105
  67.8 3.3 %all-to-all-start.1 = ((f32[4,8,512]{2,1,0:T(8,128)}), f32[4,8,512]{2,1,0:T(8,128)S(1)}, u32[]{:S(2)}, u32[]{:S(2)}) async-start(f32[4,8,512]{2,1,0:T(8,128)} %tile.2), calls=%async_computation.1 | async-start | bytes 131072 | tf_op jit(solution)/shard_map/all_to_all | solution.py:129
  71.1 5.8 %all-to-all-done.1 = f32[4,8,512]{2,1,0:T(8,128)S(1)} async-done(((f32[4,8,512]{2,1,0:T(8,128)}), f32[4,8,512]{2,1,0:T(8,128)S(1)}, u32[]{:S(2)}, u32[]{:S(2)}) %all-to-all-start.1) | async-done | bytes 65568 | tf_op jit(solution)/shard_map/all_to_all | solution.py:129
  76.9 1.3 %collective-permute-start.4 = (f32[4,512]{1,0:T(4,128)S(1)}, f32[4,512]{1,0:T(4,128)S(1)}, u32[]{:S(2)}, u32[]{:S(2)}) collective-permute-start(f32[4,512]{1,0:T(4,128)S(1)} %get-tuple-element.136), channel_id=1, source_target_pairs={{2,0},{4,2},{6,4},{3,1},{5,3},{7,5},{10,8},{12,10},{14,12},{11,9},... | collective-permute-start | bytes 24584 | tf_op jit(solution)/shard_map/ppermute | solution.py:22
  78.2 3.2 %collective-permute-start.3 = (f32[4,512]{1,0:T(4,128)S(1)}, f32[4,512]{1,0:T(4,128)S(1)}, u32[]{:S(2)}, u32[]{:S(2)}) collective-permute-start(f32[4,512]{1,0:T(4,128)S(1)} %get-tuple-element.135), channel_id=1, source_target_pairs={{0,2},{2,4},{4,6},{1,3},{3,5},{5,7},{8,10},{10,12},{12,14},{9,11},... | collective-permute-start | bytes 24584 | tf_op jit(solution)/shard_map/ppermute | solution.py:21
  82.1 1.5 %collective-permute-start.5 = (f32[4,40]{0,1:T(8,128)S(1)}, f32[4,40]{0,1:T(8,128)S(1)}, u32[]{:S(2)}, u32[]{:S(2)}) collective-permute-start(f32[4,40]{0,1:T(8,128)S(1)} %fusion.55), channel_id=1, source_target_pairs={{0,1},{1,0},{2,3},{3,2},{4,5},{5,4},{6,7},{7,6},{8,9},{9,8},{10,11... | collective-permute-start | bytes 1928 | tf_op jit(solution)/shard_map/ppermute | solution.py:41
  83.7 2.3 %collective-permute-done.5 = f32[4,40]{0,1:T(8,128)S(1)} collective-permute-done((f32[4,40]{0,1:T(8,128)S(1)}, f32[4,40]{0,1:T(8,128)S(1)}, u32[]{:S(2)}, u32[]{:S(2)}) %collective-permute-start.5) | collective-permute-done | bytes 672 | tf_op jit(solution)/shard_map/ppermute | solution.py:41
  86.7 1.3 %fusion.45 = f32[8,32,512]{2,1,0:T(8,128)S(1)} fusion(f32[8,32,520]{2,1,0:T(8,128)S(1)} %multiply_add_fusion, f32[8]{0:T(128)S(1)} %get-tuple-element.142, f32[8]{0:T(128)S(1)} %get-tuple-element.143, f32[8]{0:T(128)S(1)} %get-tuple-element.144, f32[8]{0:T(128)S(1)} %get-tuple-element.145, f32[8]{0:T(128)S(1)} %get-tuple-element.146, ...), kind=kLoop, calls=%fused_computation.103 | loop fusion | flops 2228224 | bytes 5243168 | tf_op jit(solution)/shard_map/add | solution.py:144
  88.0 0.7 subtract_select_fusion
  88.7 1.6 %copy.44 = f32[16,32,512]{2,1,0:T(8,128)} copy(f32[16,32,512]{2,0,1:T(8,128)S(1)} %subtract_select_fusion) | data formatting | bytes 2097152
  (216 shorter events, 10.4 us)
Async XLA Ops:
  2.0 5.1 %copy-start.41 = (s32[16,2]{0,1:T(2,128)S(1)}, s32[16,2]{0,1:T(2,128)}, u32[]{:S(2)}) copy-start(s32[16,2]{0,1:T(2,128)} %param.11) | copy-start | bytes 388
  2.0 5.1 %copy-start.42 = (s32[16,2]{0,1:T(2,128)S(1)}, s32[16,2]{0,1:T(2,128)}, u32[]{:S(2)}) copy-start(s32[16,2]{0,1:T(2,128)} %param.10) | copy-start | bytes 388
  2.2 9.6 %copy-start = (f32[16,32,512]{2,1,0:T(8,128)S(1)}, f32[16,32,512]{2,1,0:T(8,128)}, u32[]{:S(2)}) copy-start(f32[16,32,512]{2,1,0:T(8,128)} %param.8) | copy-start | bytes 3145732
  2.2 8.5 %collective-permute-start = (f32[16,11,512]{2,0,1:T(8,128)S(1)}, f32[16,11,512]{2,0,1:T(8,128)}, u32[]{:S(2)}, u32[]{:S(2)}) collective-permute-start(f32[16,11,512]{2,0,1:T(8,128)S(1)} %copy.47), channel_id=1, source_target_pairs={{0,2},{2,4},{4,6},{1,3},{3,5},{5,7},{8,10},{10,12},{12,14},{9,11},... | collective-permute-start | bytes 1081352 | tf_op jit(solution)/shard_map/ppermute | solution.py:21
  5.7 6.7 %collective-permute-start.1 = (f32[16,11,512]{2,0,1:T(8,128)S(1)}, f32[16,11,512]{2,0,1:T(8,128)S(1)}, u32[]{:S(2)}, u32[]{:S(2)}) collective-permute-start(f32[16,11,512]{2,0,1:T(8,128)S(1)} %copy.48), channel_id=1, source_target_pairs={{2,0},{4,2},{6,4},{3,1},{5,3},{7,5},{10,8},{12,10},{14,12},{11,9},... | collective-permute-start | bytes 1081352 | tf_op jit(solution)/shard_map/ppermute | solution.py:22
  13.0 4.5 %collective-permute-start.2 = (f32[11,864]{1,0:T(8,128)S(1)}, f32[11,864]{1,0:T(8,128)S(1)}, u32[]{:S(2)}, u32[]{:S(2)}) collective-permute-start(f32[11,864]{1,0:T(8,128)S(1)} %reshape.187), channel_id=1, source_target_pairs={{0,1},{1,0},{2,3},{3,2},{4,5},{5,4},{6,7},{7,6},{8,9},{9,8},{10,11... | collective-permute-start | bytes 114056 | tf_op jit(solution)/shard_map/ppermute | solution.py:41
  19.6 4.0 %copy-start.1 = (s32[16,32,512]{2,1,0:T(8,128)S(1)}, s32[16,32,512]{2,1,0:T(8,128)}, u32[]{:S(2)}) copy-start(s32[16,32,512]{2,1,0:T(8,128)} %param.9) | copy-start | bytes 3145732
  19.6 4.0 %copy-start.2 = (f32[16]{0:T(128)S(1)}, f32[16]{0:T(128)}, u32[]{:S(2)}) copy-start(f32[16]{0:T(128)} %get-tuple-element.57) | copy-start | bytes 196
  19.6 4.0 %copy-start.3 = (f32[16]{0:T(128)S(1)}, f32[16]{0:T(128)}, u32[]{:S(2)}) copy-start(f32[16]{0:T(128)} %get-tuple-element.58) | copy-start | bytes 196
  19.6 4.0 %copy-start.4 = (f32[16]{0:T(128)S(1)}, f32[16]{0:T(128)}, u32[]{:S(2)}) copy-start(f32[16]{0:T(128)} %get-tuple-element.59) | copy-start | bytes 196
  19.6 4.0 %copy-start.5 = (f32[16]{0:T(128)S(1)}, f32[16]{0:T(128)}, u32[]{:S(2)}) copy-start(f32[16]{0:T(128)} %get-tuple-element.60) | copy-start | bytes 196
  19.6 4.0 %copy-start.6 = (f32[16]{0:T(128)S(1)}, f32[16]{0:T(128)}, u32[]{:S(2)}) copy-start(f32[16]{0:T(128)} %get-tuple-element.61) | copy-start | bytes 196
  19.6 4.0 %copy-start.7 = (f32[16]{0:T(128)S(1)}, f32[16]{0:T(128)}, u32[]{:S(2)}) copy-start(f32[16]{0:T(128)} %get-tuple-element.62) | copy-start | bytes 196
  19.7 4.0 %copy-start.8 = (f32[16]{0:T(128)S(1)}, f32[16]{0:T(128)}, u32[]{:S(2)}) copy-start(f32[16]{0:T(128)} %get-tuple-element.63) | copy-start | bytes 196
  19.7 4.0 %copy-start.9 = (f32[16]{0:T(128)S(1)}, f32[16]{0:T(128)}, u32[]{:S(2)}) copy-start(f32[16]{0:T(128)} %get-tuple-element.64) | copy-start | bytes 196
  19.7 4.0 %copy-start.10 = (f32[16]{0:T(128)S(1)}, f32[16]{0:T(128)}, u32[]{:S(2)}) copy-start(f32[16]{0:T(128)} %get-tuple-element.65) | copy-start | bytes 196
  19.7 4.0 %copy-start.11 = (f32[16]{0:T(128)S(1)}, f32[16]{0:T(128)}, u32[]{:S(2)}) copy-start(f32[16]{0:T(128)} %get-tuple-element.66) | copy-start | bytes 196
  19.7 4.0 %copy-start.12 = (f32[16]{0:T(128)S(1)}, f32[16]{0:T(128)}, u32[]{:S(2)}) copy-start(f32[16]{0:T(128)} %get-tuple-element.67) | copy-start | bytes 196
  30.8 31.8 %all-to-all-start = ((f32[16,32,512]{2,0,1:T(8,128)}), f32[16,32,512]{2,0,1:T(8,128)S(1)}, u32[]{:S(2)}, u32[]{:S(2)}) async-start(f32[16,32,512]{2,0,1:T(8,128)} %get-tuple-element.113), calls=%async_computation | async-start | bytes 2097152 | tf_op jit(solution)/shard_map/all_to_all | solution.py:127
  67.0 14.4 %copy-start.43 = (s32[16]{0:T(128)S(1)}, s32[16]{0:T(128)}, u32[]{:S(2)}) copy-start(s32[16]{0:T(128)} %param.12) | copy-start | bytes 196
  67.8 9.1 %all-to-all-start.1 = ((f32[4,8,512]{2,1,0:T(8,128)}), f32[4,8,512]{2,1,0:T(8,128)S(1)}, u32[]{:S(2)}, u32[]{:S(2)}) async-start(f32[4,8,512]{2,1,0:T(8,128)} %tile.2), calls=%async_computation.1 | async-start | bytes 131072 | tf_op jit(solution)/shard_map/all_to_all | solution.py:129
  76.9 4.5 %collective-permute-start.4 = (f32[4,512]{1,0:T(4,128)S(1)}, f32[4,512]{1,0:T(4,128)S(1)}, u32[]{:S(2)}, u32[]{:S(2)}) collective-permute-start(f32[4,512]{1,0:T(4,128)S(1)} %get-tuple-element.136), channel_id=1, source_target_pairs={{2,0},{4,2},{6,4},{3,1},{5,3},{7,5},{10,8},{12,10},{14,12},{11,9},... | collective-permute-start | bytes 24584 | tf_op jit(solution)/shard_map/ppermute | solution.py:22
  78.2 3.8 %collective-permute-start.3 = (f32[4,512]{1,0:T(4,128)S(1)}, f32[4,512]{1,0:T(4,128)S(1)}, u32[]{:S(2)}, u32[]{:S(2)}) collective-permute-start(f32[4,512]{1,0:T(4,128)S(1)} %get-tuple-element.135), channel_id=1, source_target_pairs={{0,2},{2,4},{4,6},{1,3},{3,5},{5,7},{8,10},{10,12},{12,14},{9,11},... | collective-permute-start | bytes 24584 | tf_op jit(solution)/shard_map/ppermute | solution.py:21
  82.1 3.8 %collective-permute-start.5 = (f32[4,40]{0,1:T(8,128)S(1)}, f32[4,40]{0,1:T(8,128)S(1)}, u32[]{:S(2)}, u32[]{:S(2)}) collective-permute-start(f32[4,40]{0,1:T(8,128)S(1)} %fusion.55), channel_id=1, source_target_pairs={{0,1},{1,0},{2,3},{3,2},{4,5},{5,4},{6,7},{7,6},{8,9},{9,8},{10,11... | collective-permute-start | bytes 1928 | tf_op jit(solution)/shard_map/ppermute | solution.py:41
  (28 other events, 45.8 us)
where the time goes:
time: 91.4 us; the launch traced here: 90.9 us
  waiting for transfers between devices  36.9 us (40%)
  starting transfers between devices  21.6 us (24%)
  other arithmetic  18.2 us (20%)
  local copies, waits for them, and re-layouts  11.5 us (13%)
  between operations  1.6 us (2%)
    all_to_all x1, waiting for transfers between devices, body(): lax.all_to_all(flagged, 'exp', split_axis=1, concat_axis=0, tiled=True)  26.2 us
    select_n x1, other arithmetic, body(): flagged = jnp.where(bad_pixels == 1, sentinel, warped)  6.99 us
    ppermute x2, starting transfers between devices, _row_halo(): lax.ppermute(lax.slice_in_dim(block, size - width, None, axis=dim), 'row'...  6.48 us
    all_to_all x1, waiting for transfers between devices, body(): lax.all_to_all(jnp.tile(band, (groups, 1)), 'exp', split_axis=0, concat_a...  5.8 us
    all_to_all x1, starting transfers between devices, body(): lax.all_to_all(flagged, 'exp', split_axis=1, concat_axis=0, tiled=True)  5.4 us
    unnamed x94, local copies, waits for them, and re-layouts  4.46 us
    ppermute x2, waiting for transfers between devices, _col_halo(): arrived = lax.ppermute(packed, 'col', [(0, 1), (1, 0)])  4.23 us
    ppermute x2, starting transfers between devices, _col_halo(): arrived = lax.ppermute(packed, 'col', [(0, 1), (1, 0)])  3.87 us
  transfers between devices with their start and end apart: 8, of which 5 were waited for; matrix products, arithmetic and copies ran while one was open for 7% of the time, Pallas kernels for 0%

commit v1 on v0

--- a/solution.py
+++ b/solution.py
@@ -11,6 +11,30 @@
 sentinel = 1000000.0
 half_sentinel = 500000.0
 pivot_span = 16.0
+
+
+def in_blocks(value, dim, size):
+    lengths = value.shape
+    tiles = value.reshape(*lengths[:dim], size, lengths[dim] // size, *lengths[dim + 1 :])
+    return jnp.moveaxis(tiles, dim, 0)
+
+
+def joined_along(pieces, dim):
+    dims = list(pieces.shape[1:])
+    dims[dim] *= pieces.shape[0]
+    return jnp.moveaxis(pieces, 0, dim).reshape(dims)
+
+
+def rotated_exchange(x, axis, split_dim, concat_dim):
+    peers, index = (lax.axis_size(axis), lax.axis_index(axis))
+    blocks = in_blocks(x, split_dim, peers)
+    out = blocks
+    for step in range(1, peers):
+        target, source = ((index + step) % peers, (index - step) % peers)
+        sent = lax.dynamic_index_in_dim(blocks, target, 0)
+        theirs = lax.ppermute(sent, axis, [(i, (i + step) % peers) for i in range(peers)])
+        out = lax.dynamic_update_slice_in_dim(out, theirs, source, axis=0)
+    return joined_along(out, concat_dim)
 
 
 def _row_halo(block, dim, width):
@@ -126,9 +150,7 @@
     flagged = jnp.where(bad_pixels == 1, sentinel, warped)
     band = stack_median(lax.all_to_all(flagged, "exp", split_axis=1, concat_axis=0, tiled=True))
     groups = lax.axis_size("exp")
-    median_sky = lax.all_to_all(
-        jnp.tile(band, (groups, 1)), "exp", split_axis=0, concat_axis=0, tiled=True
-    )
+    median_sky = rotated_exchange(jnp.tile(band, (groups, 1)), "exp", 0, 0)
     bordered = extended(median_sky, 0, 1, PSF_RADIUS)
     blur = blur_table()
     taps = 2 * PSF_RADIUS + 1

time: 91.4 us -> 87.1 us (0.953)
  waiting for transfers between devices: 36.9 us -> 33.2 us
  local copies, waits for them, and re-layouts: 11.5 us -> 10.3 us
    all_to_all x1 -> x0, waiting for transfers between devices: 5.8 us -> none  [body(): lax.all_to_all(jnp.tile(band, (groups, 1)), 'exp', split_axis=0, concat_a...]
    ppermute x0 -> x3, starting transfers between devices: none -> 3.85 us  [rotated_exchange(): lax.ppermute(sent, axis, [(i, (i + step) % peers) for i in range(peers)])]
    all_to_all x1 -> x0, starting transfers between devices: 3.28 us -> none  [body(): lax.all_to_all(jnp.tile(band, (groups, 1)), 'exp', split_axis=0, concat_a...]
    ppermute x0 -> x3, waiting for transfers between devices: none -> 2.18 us  [rotated_exchange(): lax.ppermute(sent, axis, [(i, (i + step) % peers) for i in range(peers)])]
    unnamed x94 -> x95, local copies, waits for them, and re-layouts: 4.46 us -> 3.83 us
  transfers between devices with their start and end apart: 8 -> 10, of which waited for: 5 -> 6; matrix products, arithmetic and copies ran while one was open for 7% -> 7% of each run, Pallas kernels for 0% -> 0%
where the time goes in v1:
time: 87.1 us; the launch traced here: 86.8 us
  waiting for transfers between devices  33.2 us (38%)
  starting transfers between devices  22.2 us (25%)
  other arithmetic  18.2 us (21%)
  local copies, waits for them, and re-layouts  10.3 us (12%)
  between operations  1.7 us (2%)
    all_to_all x1, waiting for transfers between devices, body(): lax.all_to_all(flagged, 'exp', split_axis=1, concat_axis=0, tiled=True)  26.2 us
    select_n x1, other arithmetic, body(): flagged = jnp.where(bad_pixels == 1, sentinel, warped)  6.99 us
    ppermute x2, starting transfers between devices, _row_halo(): lax.ppermute(lax.slice_in_dim(block, size - width, None, axis=dim), 'row'...  6.48 us
    all_to_all x1, starting transfers between devices, body(): lax.all_to_all(flagged, 'exp', split_axis=1, concat_axis=0, tiled=True)  5.4 us
    ppermute x2, waiting for transfers between devices, _col_halo(): arrived = lax.ppermute(packed, 'col', [(0, 1), (1, 0)])  4.23 us
    ppermute x2, starting transfers between devices, _col_halo(): arrived = lax.ppermute(packed, 'col', [(0, 1), (1, 0)])  3.87 us
    add x1, other arithmetic, resample_axis(): total = total + coefficients[:, position, None, None] * window  3.86 us
    ppermute x3, starting transfers between devices, rotated_exchange(): lax.ppermute(sent, axis, [(i, (i + step) % peers) for i in range(peers)])  3.85 us
  transfers between devices with their start and end apart: 10, of which 6 were waited for; matrix products, arithmetic and copies ran while one was open for 7% of the time, Pallas kernels for 0%

profile of v1, /device:TPU:0, one launch (start us, length us, event | category | flops | bytes accessed | tf_op | source)
XLA Modules:
  0.0 86.8 jit_solution(13438009576152646613)
XLA Ops:
  0.6 1.3 %fusion.134 = (f32[16,11,512]{2,1,0:T(8,128)S(1)}, f32[16,11,512]{2,1,0:T(8,128)S(1)}) fusion(f32[16,32,512]{2,1,0:T(8,128)} %param.8), kind=kLoop, calls=%fused_computation.318 | loop fusion | bytes 1441792 | tf_op jit(solution)/shard_map/slice | solution.py:46
  2.2 3.3 %collective-permute-start = (f32[16,11,512]{2,0,1:T(8,128)S(1)}, f32[16,11,512]{2,0,1:T(8,128)}, u32[]{:S(2)}, u32[]{:S(2)}) collective-permute-start(f32[16,11,512]{2,0,1:T(8,128)S(1)} %copy.47), channel_id=1, source_target_pairs={{0,2},{2,4},{4,6},{1,3},{3,5},{5,7},{8,10},{10,12},{12,14},{9,11},... | collective-permute-start | bytes 1081352 | tf_op jit(solution)/shard_map/ppermute | solution.py:45
  5.7 1.3 %collective-permute-start.1 = (f32[16,11,512]{2,0,1:T(8,128)S(1)}, f32[16,11,512]{2,0,1:T(8,128)S(1)}, u32[]{:S(2)}, u32[]{:S(2)}) collective-permute-start(f32[16,11,512]{2,0,1:T(8,128)S(1)} %copy.48), channel_id=1, source_target_pairs={{2,0},{4,2},{6,4},{3,1},{5,3},{7,5},{10,8},{12,10},{14,12},{11,9},... | collective-permute-start | bytes 1081352 | tf_op jit(solution)/shard_map/ppermute | solution.py:46
  7.7 0.8 slice_reduce_fusion.43
  8.5 1.1 %slice_reduce_fusion.44 = (f32[16]{0:T(128)}, f32[16]{0:T(128)}, f32[16]{0:T(128)}, f32[16]{0:T(128)}, f32[16]{0:T(128)}, /*index=5*/f32[16]{0:T(128)}, f32[16]{...) fusion(f32[16,23]{1,0:T(8,128)S(1)} %select_reduce_fusion), kind=kLoop, calls=%fused_computation.204 | loop fusion | bytes 2432 | tf_op jit(solution)/shard_map/slice | solution.py:113
  9.7 1.1 %slice_reduce_fusion.45 = (f32[16]{0:T(128)S(1)}, f32[16]{0:T(128)S(1)}, f32[16]{0:T(128)}, f32[16]{0:T(128)}, f32[16]{0:T(128)}, /*index=5*/f32[16]{0:T(128)}, ...) fusion(f32[16,23]{1,0:T(8,128)S(1)} %select_reduce_fusion.1), kind=kLoop, calls=%fused_computation.205 | loop fusion | bytes 2432 | tf_op jit(solution)/shard_map/slice | solution.py:113
  10.7 1.0 %constant_dynamic-update-slice_fusion.2 = f32[16,54,512]{2,0,1:T(8,128)S(1)} fusion(f32[16,11,512]{2,0,1:T(8,128)} %collective-permute-done), kind=kLoop, calls=%fused_computation.208 | loop fusion | bytes 720896
  13.0 2.4 %collective-permute-start.2 = (f32[11,864]{1,0:T(8,128)S(1)}, f32[11,864]{1,0:T(8,128)S(1)}, u32[]{:S(2)}, u32[]{:S(2)}) collective-permute-start(f32[11,864]{1,0:T(8,128)S(1)} %reshape.189), channel_id=1, source_target_pairs={{0,1},{1,0},{2,3},{3,2},{4,5},{5,4},{6,7},{7,6},{8,9},{9,8},{10,11... | collective-permute-start | bytes 114056 | tf_op jit(solution)/shard_map/ppermute | solution.py:65
  15.6 1.9 %collective-permute-done.2 = f32[11,864]{1,0:T(8,128)S(1)} collective-permute-done((f32[11,864]{1,0:T(8,128)S(1)}, f32[11,864]{1,0:T(8,128)S(1)}, u32[]{:S(2)}, u32[]{:S(2)}) %collective-permute-start.2) | collective-permute-done | bytes 38048 | tf_op jit(solution)/shard_map/ppermute | solution.py:65
  18.6 0.7 pad_maximum_fusion
  19.8 3.9 %fusion = f32[16,32,534]{2,0,1:T(8,128)S(1)} fusion(f32[16,54,534]{2,0,1:T(8,128)S(1)} %pad_maximum_fusion, f32[16]{0:T(128)S(1)} %copy-done.25, f32[16]{0:T(128)S(1)} %copy-done.26, f32[16]{0:T(128)S(1)} %copy-done.27, f32[16]{0:T(128)S(1)} %copy-done.28, f32[16]{0:T(128)S(1)} %copy-done.29, f32[16]{0:T(128)S(1)} %copy-done.30, f32[16]{0:T(128)S(1)} %copy-done.31, ...), kind=kLoop, calls=%fused_computation.8 | loop fusion | flops 12303360 | bytes 26248640 | tf_op jit(solution)/shard_map/add | solution.py:113
  23.8 7.0 %broadcast_select_fusion = (f32[16,32,512]{2,0,1:T(8,128)}, f32[16,32,512]{2,0,1:T(8,128)S(1)}, pred[16,32,512]{2,0,1:T(8,128)(4,1)S(1)}) fusion(f32[16,32,534]{2,0,1:T(8,128)S(1)} %fusion, f32[16]{0:T(128)S(1)} %get-tuple-element.56, f32[16]{0:T(128)S(1)} %copy-done.3, f32[16]{0:T(128)S(1)} %copy-done.4, f32[16]{0:T(128)S(1)} %copy-done.5, ...), kind=kLoop, calls=%fused_computation.119 | loop fusion | flops 12320768 | bytes 27526592 | tf_op jit(solution)/shard_map/jit(_where)/select_n | solution.py:150
  30.8 5.4 %all-to-all-start = ((f32[16,32,512]{2,0,1:T(8,128)}), f32[16,32,512]{2,0,1:T(8,128)S(1)}, u32[]{:S(2)}, u32[]{:S(2)}) async-start(f32[16,32,512]{2,0,1:T(8,128)} %get-tuple-element.113), calls=%async_computation | async-start | bytes 2097152 | tf_op jit(solution)/shard_map/all_to_all | solution.py:151
  36.4 26.2 %all-to-all-done = f32[16,32,512]{2,0,1:T(8,128)S(1)} async-done(((f32[16,32,512]{2,0,1:T(8,128)}), f32[16,32,512]{2,0,1:T(8,128)S(1)}, u32[]{:S(2)}, u32[]{:S(2)}) %all-to-all-start) | async-done | bytes 1048608 | tf_op jit(solution)/shard_map/all_to_all | solution.py:151
  63.4 3.6 %while.13 = (s32[]{:T(128)}, f32[8,512]{1,0:T(8,128)S(1)}, f32[8,512]{1,0:T(8,128)S(1)}, f32[64,8,512]{2,1,0:T(8,128)S(1)}, f32[8,512]{1,0:T(8,128)S(1)}, /*index=5*/s32[]{:T(128)}, s32[]{:T(128)}) while((s32[]{:T(128)}, f32[8,512]{1,0:T(8,128)S(1)}, f32[8,512]{1,0:T(8,128)S(1)}, f32[64,8,512]{2,1,0:T(8,128)S(1)}, ...), condition=%wide.region_7.9_spmd.clone, body=%wide.region_5.8_spmd.clone.sunk | while | flops 1110019 | bytes 1302625 | solution.py:129
  67.3 1.9 %collective-permute-start.4 = (f32[1,8,512]{2,1,0:T(8,128)S(1)}, f32[1,8,512]{2,1,0:T(8,128)S(1)}, u32[]{:S(2)}, u32[]{:S(2)}) collective-permute-start(f32[1,8,512]{2,1,0:T(8,128)S(1)} %bitcast.85), channel_id=1, source_target_pairs={{0,16},{8,24},{16,0},{24,8},{1,17},{9,25},{17,1},{25,9},{2,18},{10... | collective-permute-start | bytes 49160 | tf_op jit(solution)/shard_map/ppermute | solution.py:35
  69.3 1.9 %collective-permute-start.5 = (f32[1,8,512]{2,1,0:T(8,128)S(1)}, f32[1,8,512]{2,1,0:T(8,128)S(1)}, u32[]{:S(2)}, u32[]{:S(2)}) collective-permute-start(f32[1,8,512]{2,1,0:T(8,128)S(1)} %bitcast.86), channel_id=1, source_target_pairs={{0,24},{8,0},{16,8},{24,16},{1,25},{9,1},{17,9},{25,17},{2,26},{10... | collective-permute-start | bytes 49160 | tf_op jit(solution)/shard_map/ppermute | solution.py:35
  71.1 1.8 %collective-permute-done.3 = f32[1,8,512]{2,1,0:T(8,128)S(1)} collective-permute-done((f32[1,8,512]{2,1,0:T(8,128)S(1)}, f32[1,8,512]{2,1,0:T(8,128)S(1)}, u32[]{:S(2)}, u32[]{:S(2)}) %collective-permute-start.3) | collective-permute-done | bytes 16416 | tf_op jit(solution)/shard_map/ppermute | solution.py:35
  73.4 1.3 %collective-permute-start.7 = (f32[4,512]{1,0:T(4,128)S(1)}, f32[4,512]{1,0:T(4,128)S(1)}, u32[]{:S(2)}, u32[]{:S(2)}) collective-permute-start(f32[4,512]{1,0:T(4,128)S(1)} %get-tuple-element.136), channel_id=1, source_target_pairs={{2,0},{4,2},{6,4},{3,1},{5,3},{7,5},{10,8},{12,10},{14,12},{11,9},... | collective-permute-start | bytes 24584 | tf_op jit(solution)/shard_map/ppermute | solution.py:46
  74.7 3.2 %collective-permute-start.6 = (f32[4,512]{1,0:T(4,128)S(1)}, f32[4,512]{1,0:T(4,128)S(1)}, u32[]{:S(2)}, u32[]{:S(2)}) collective-permute-start(f32[4,512]{1,0:T(4,128)S(1)} %get-tuple-element.135), channel_id=1, source_target_pairs={{0,2},{2,4},{4,6},{1,3},{3,5},{5,7},{8,10},{10,12},{12,14},{9,11},... | collective-permute-start | bytes 24584 | tf_op jit(solution)/shard_map/ppermute | solution.py:45
  78.6 1.5 %collective-permute-start.8 = (f32[4,40]{0,1:T(8,128)S(1)}, f32[4,40]{0,1:T(8,128)S(1)}, u32[]{:S(2)}, u32[]{:S(2)}) collective-permute-start(f32[4,40]{0,1:T(8,128)S(1)} %fusion.55), channel_id=1, source_target_pairs={{0,1},{1,0},{2,3},{3,2},{4,5},{5,4},{6,7},{7,6},{8,9},{9,8},{10,11... | collective-permute-start | bytes 1928 | tf_op jit(solution)/shard_map/ppermute | solution.py:65
  80.1 2.3 %collective-permute-done.8 = f32[4,40]{0,1:T(8,128)S(1)} collective-permute-done((f32[4,40]{0,1:T(8,128)S(1)}, f32[4,40]{0,1:T(8,128)S(1)}, u32[]{:S(2)}, u32[]{:S(2)}) %collective-permute-start.8) | collective-permute-done | bytes 672 | tf_op jit(solution)/shard_map/ppermute | solution.py:65
  83.2 1.3 %fusion.45 = f32[8,32,512]{2,1,0:T(8,128)S(1)} fusion(f32[8,32,520]{2,1,0:T(8,128)S(1)} %multiply_add_fusion, f32[8]{0:T(128)S(1)} %get-tuple-element.142, f32[8]{0:T(128)S(1)} %get-tuple-element.143, f32[8]{0:T(128)S(1)} %get-tuple-element.144, f32[8]{0:T(128)S(1)} %get-tuple-element.145, f32[8]{0:T(128)S(1)} %get-tuple-element.146, ...), kind=kLoop, calls=%fused_computation.103 | loop fusion | flops 2228224 | bytes 5243168 | tf_op jit(solution)/shard_map/add | solution.py:166
  85.2 1.6 %copy.44 = f32[16,32,512]{2,1,0:T(8,128)} copy(f32[16,32,512]{2,0,1:T(8,128)S(1)} %subtract_select_fusion) | data formatting | bytes 2097152
  (224 shorter events, 10.3 us)
Async XLA Ops:
  2.0 5.1 %copy-start.42 = (s32[16,2]{0,1:T(2,128)S(1)}, s32[16,2]{0,1:T(2,128)}, u32[]{:S(2)}) copy-start(s32[16,2]{0,1:T(2,128)} %param.11) | copy-start | bytes 388
  2.0 5.1 %copy-start.43 = (s32[16,2]{0,1:T(2,128)S(1)}, s32[16,2]{0,1:T(2,128)}, u32[]{:S(2)}) copy-start(s32[16,2]{0,1:T(2,128)} %param.10) | copy-start | bytes 388
  2.2 9.6 %copy-start = (f32[16,32,512]{2,1,0:T(8,128)S(1)}, f32[16,32,512]{2,1,0:T(8,128)}, u32[]{:S(2)}) copy-start(f32[16,32,512]{2,1,0:T(8,128)} %param.8) | copy-start | bytes 3145732
  2.2 8.5 %collective-permute-start = (f32[16,11,512]{2,0,1:T(8,128)S(1)}, f32[16,11,512]{2,0,1:T(8,128)}, u32[]{:S(2)}, u32[]{:S(2)}) collective-permute-start(f32[16,11,512]{2,0,1:T(8,128)S(1)} %copy.47), channel_id=1, source_target_pairs={{0,2},{2,4},{4,6},{1,3},{3,5},{5,7},{8,10},{10,12},{12,14},{9,11},... | collective-permute-start | bytes 1081352 | tf_op jit(solution)/shard_map/ppermute | solution.py:45
  5.7 6.7 %collective-permute-start.1 = (f32[16,11,512]{2,0,1:T(8,128)S(1)}, f32[16,11,512]{2,0,1:T(8,128)S(1)}, u32[]{:S(2)}, u32[]{:S(2)}) collective-permute-start(f32[16,11,512]{2,0,1:T(8,128)S(1)} %copy.48), channel_id=1, source_target_pairs={{2,0},{4,2},{6,4},{3,1},{5,3},{7,5},{10,8},{12,10},{14,12},{11,9},... | collective-permute-start | bytes 1081352 | tf_op jit(solution)/shard_map/ppermute | solution.py:46
  13.0 4.5 %collective-permute-start.2 = (f32[11,864]{1,0:T(8,128)S(1)}, f32[11,864]{1,0:T(8,128)S(1)}, u32[]{:S(2)}, u32[]{:S(2)}) collective-permute-start(f32[11,864]{1,0:T(8,128)S(1)} %reshape.189), channel_id=1, source_target_pairs={{0,1},{1,0},{2,3},{3,2},{4,5},{5,4},{6,7},{7,6},{8,9},{9,8},{10,11... | collective-permute-start | bytes 114056 | tf_op jit(solution)/shard_map/ppermute | solution.py:65
  19.6 4.0 %copy-start.1 = (s32[16,32,512]{2,1,0:T(8,128)S(1)}, s32[16,32,512]{2,1,0:T(8,128)}, u32[]{:S(2)}) copy-start(s32[16,32,512]{2,1,0:T(8,128)} %param.9) | copy-start | bytes 3145732
  19.6 4.0 %copy-start.3 = (f32[16]{0:T(128)S(1)}, f32[16]{0:T(128)}, u32[]{:S(2)}) copy-start(f32[16]{0:T(128)} %get-tuple-element.57) | copy-start | bytes 196
  19.6 4.0 %copy-start.4 = (f32[16]{0:T(128)S(1)}, f32[16]{0:T(128)}, u32[]{:S(2)}) copy-start(f32[16]{0:T(128)} %get-tuple-element.58) | copy-start | bytes 196
  19.6 4.0 %copy-start.5 = (f32[16]{0:T(128)S(1)}, f32[16]{0:T(128)}, u32[]{:S(2)}) copy-start(f32[16]{0:T(128)} %get-tuple-element.59) | copy-start | bytes 196
  19.6 4.0 %copy-start.6 = (f32[16]{0:T(128)S(1)}, f32[16]{0:T(128)}, u32[]{:S(2)}) copy-start(f32[16]{0:T(128)} %get-tuple-element.60) | copy-start | bytes 196
  19.6 4.0 %copy-start.7 = (f32[16]{0:T(128)S(1)}, f32[16]{0:T(128)}, u32[]{:S(2)}) copy-start(f32[16]{0:T(128)} %get-tuple-element.61) | copy-start | bytes 196
  19.6 4.0 %copy-start.8 = (f32[16]{0:T(128)S(1)}, f32[16]{0:T(128)}, u32[]{:S(2)}) copy-start(f32[16]{0:T(128)} %get-tuple-element.62) | copy-start | bytes 196
  19.7 4.0 %copy-start.9 = (f32[16]{0:T(128)S(1)}, f32[16]{0:T(128)}, u32[]{:S(2)}) copy-start(f32[16]{0:T(128)} %get-tuple-element.63) | copy-start | bytes 196
  19.7 4.0 %copy-start.10 = (f32[16]{0:T(128)S(1)}, f32[16]{0:T(128)}, u32[]{:S(2)}) copy-start(f32[16]{0:T(128)} %get-tuple-element.64) | copy-start | bytes 196
  30.8 31.8 %all-to-all-start = ((f32[16,32,512]{2,0,1:T(8,128)}), f32[16,32,512]{2,0,1:T(8,128)S(1)}, u32[]{:S(2)}, u32[]{:S(2)}) async-start(f32[16,32,512]{2,0,1:T(8,128)} %get-tuple-element.113), calls=%async_computation | async-start | bytes 2097152 | tf_op jit(solution)/shard_map/all_to_all | solution.py:151
  67.0 10.9 %copy-start.44 = (s32[16]{0:T(128)S(1)}, s32[16]{0:T(128)}, u32[]{:S(2)}) copy-start(s32[16]{0:T(128)} %param.12) | copy-start | bytes 196
  67.2 5.7 %collective-permute-start.3 = (f32[1,8,512]{2,1,0:T(8,128)S(1)}, f32[1,8,512]{2,1,0:T(8,128)S(1)}, u32[]{:S(2)}, u32[]{:S(2)}) collective-permute-start(f32[1,8,512]{2,1,0:T(8,128)S(1)} %bitcast.84), channel_id=1, source_target_pairs={{0,8},{8,16},{16,24},{24,0},{1,9},{9,17},{17,25},{25,1},{2,10},{10... | collective-permute-start | bytes 49160 | tf_op jit(solution)/shard_map/ppermute | solution.py:35
  67.3 5.6 %collective-permute-start.4 = (f32[1,8,512]{2,1,0:T(8,128)S(1)}, f32[1,8,512]{2,1,0:T(8,128)S(1)}, u32[]{:S(2)}, u32[]{:S(2)}) collective-permute-start(f32[1,8,512]{2,1,0:T(8,128)S(1)} %bitcast.85), channel_id=1, source_target_pairs={{0,16},{8,24},{16,0},{24,8},{1,17},{9,25},{17,1},{25,9},{2,18},{10... | collective-permute-start | bytes 49160 | tf_op jit(solution)/shard_map/ppermute | solution.py:35
  69.3 4.1 %collective-permute-start.5 = (f32[1,8,512]{2,1,0:T(8,128)S(1)}, f32[1,8,512]{2,1,0:T(8,128)S(1)}, u32[]{:S(2)}, u32[]{:S(2)}) collective-permute-start(f32[1,8,512]{2,1,0:T(8,128)S(1)} %bitcast.86), channel_id=1, source_target_pairs={{0,24},{8,0},{16,8},{24,16},{1,25},{9,1},{17,9},{25,17},{2,26},{10... | collective-permute-start | bytes 49160 | tf_op jit(solution)/shard_map/ppermute | solution.py:35
  73.3 9.8 %copy-start.2 = (f32[4,8,512]{2,1,0:T(8,128)}, f32[4,8,512]{2,1,0:T(8,128)S(1)}, u32[]{:S(2)}) copy-start(f32[4,8,512]{2,1,0:T(8,128)S(1)} %constant_dynamic-update-slice_fusion.3) | copy-start | bytes 196612
  73.4 4.5 %collective-permute-start.7 = (f32[4,512]{1,0:T(4,128)S(1)}, f32[4,512]{1,0:T(4,128)S(1)}, u32[]{:S(2)}, u32[]{:S(2)}) collective-permute-start(f32[4,512]{1,0:T(4,128)S(1)} %get-tuple-element.136), channel_id=1, source_target_pairs={{2,0},{4,2},{6,4},{3,1},{5,3},{7,5},{10,8},{12,10},{14,12},{11,9},... | collective-permute-start | bytes 24584 | tf_op jit(solution)/shard_map/ppermute | solution.py:46
  74.7 3.8 %collective-permute-start.6 = (f32[4,512]{1,0:T(4,128)S(1)}, f32[4,512]{1,0:T(4,128)S(1)}, u32[]{:S(2)}, u32[]{:S(2)}) collective-permute-start(f32[4,512]{1,0:T(4,128)S(1)} %get-tuple-element.135), channel_id=1, source_target_pairs={{0,2},{2,4},{4,6},{1,3},{3,5},{5,7},{8,10},{10,12},{12,14},{9,11},... | collective-permute-start | bytes 24584 | tf_op jit(solution)/shard_map/ppermute | solution.py:45
  78.6 3.8 %collective-permute-start.8 = (f32[4,40]{0,1:T(8,128)S(1)}, f32[4,40]{0,1:T(8,128)S(1)}, u32[]{:S(2)}, u32[]{:S(2)}) collective-permute-start(f32[4,40]{0,1:T(8,128)S(1)} %fusion.55), channel_id=1, source_target_pairs={{0,1},{1,0},{2,3},{3,2},{4,5},{5,4},{6,7},{7,6},{8,9},{9,8},{10,11... | collective-permute-start | bytes 1928 | tf_op jit(solution)/shard_map/ppermute | solution.py:65
  (31 other events, 57.9 us)
